TPU v7x, 256 devices: a whole 4x4x8 slice. The times are simulated.
256 devices in a mesh: tm: 64 (over y, z, core), state: 4 (over x).
Axes of the slice: x: 4, y: 4, z: 8, core: 2. Of those that a mesh axis runs over, the one named last changes fastest.
Arguments:
- dynamics: float32 [512, 512], P('state'), may hold values from -1 to 1
- pattern: int32 [4, 4], replicated, may hold values from 0 to 1
- initial_mean: float32 [4, 512], replicated, may hold values from -6 to 6
- observed: float32 [1024, 4], P('tm'), may hold values from -6 to 6
- obs_index: int32 [1024], P('tm'), may hold values from 0 to 511
- obs_noise: float32 [1024], P('tm'), may hold values from 0.5 to 4
Outputs:
- filtered: float32 [1024, 4, 512], P('tm', 'state')
- smoothed: float32 [1024, 4, 512], P('tm', 'state')
All inputs are finite; a program needn't handle non-finite values.
Results may differ from a plain program's by a relative error of at most 0.0003.
Values sent between devices are 32-bit elements; how exact they have to be, the bound alone decides.
No kernel may reach another device: no remote copies, remote signals or barrier semaphores. Data moves between devices by JAX's collectives and lax.ppermute only.
A program may use at most 256 MiB of HBM per device.

v0:
```python
import jax
import jax.numpy as jnp
from jax import lax
from jax.sharding import PartitionSpec as P

AXES = ("tm", "state")


def product(left, right):
    return jnp.dot(left, right, precision=lax.Precision.HIGHEST, preferred_element_type=jnp.float32)


def transposed(left, right):
    return lax.dot_general(
        left,
        right,
        (((1,), (1,)), ((), ())),
        precision=lax.Precision.HIGHEST,
        preferred_element_type=jnp.float32,
    )


def leading(left, right):
    return lax.dot_general(
        left,
        right,
        (((0,), (0,)), ((), ())),
        precision=lax.Precision.HIGHEST,
        preferred_element_type=jnp.float32,
    )


def shifted(block, distance, total):
    route = [(i, i + distance) for i in range(total) if 0 <= i + distance < total]
    return lax.ppermute(block, AXES, route)


def per_device(dynamics, pattern, initial_mean, observed, obs_index, obs_noise):
    state_width = dynamics.shape[1]
    blocks = pattern.shape[0]
    block_span = state_width // blocks
    seq_total = initial_mean.shape[0]
    members = lax.axis_size("state")
    segments = lax.axis_size("tm") * members
    member = lax.axis_index("state")
    segment = lax.axis_index(AXES)
    span = observed.shape[0] // members
    steps_total = span * segments
    present = jnp.maximum(pattern, jnp.eye(blocks, dtype=jnp.int32))
    block_mask = jnp.repeat(jnp.repeat(present, block_span, 0), block_span, 1).astype(jnp.float32)
    transition = lax.all_gather(dynamics, "state", axis=0, tiled=True) * block_mask
    first = member * span
    obs_here = lax.dynamic_slice_in_dim(observed, first, span, 0)
    index_here = lax.dynamic_slice_in_dim(obs_index, first, span, 0)
    noise_here = lax.dynamic_slice_in_dim(obs_noise, first, span, 0)
    gains = 1.0 / (1.0 + noise_here)
    state_index = jnp.arange(state_width, dtype=jnp.int32)
    hits = (state_index[None, :] == index_here[:, None]).astype(jnp.float32)
    scales = 1.0 - gains[:, None] * hits
    global_step = segment * span + jnp.arange(span, dtype=jnp.int32)
    keeps = jnp.where(global_step == steps_total - 1, 0.0, 1.0).astype(jnp.float32)
    pushes = [(gains[j] * obs_here[j])[:, None] * hits[j][None, :] for j in range(span)]
    filt_a = transition * scales[0][:, None]
    filt_b = pushes[0]
    for j in range(1, span):
        filt_a = product(transition, filt_a) * scales[j][:, None]
        filt_b = transposed(filt_b, transition) * scales[j][None, :] + pushes[j]
    last = span - 1
    smooth_q = keeps[last] * (transition.T * scales[last][:, None])
    for j in range(last - 1, -1, -1):
        smooth_q = keeps[j] * (leading(transition, smooth_q) * scales[j][:, None])
    levels = 0
    while 2 ** (levels + 1) < segments:
        levels += 1
    stored_q = []
    for level in range(levels):
        distance = 2**level
        arrived_a, arrived_b = shifted((filt_a, filt_b), distance, segments)
        arrived_q = shifted(smooth_q, -distance, segments)
        usable = segment >= distance
        new_a = product(filt_a, arrived_a)
        new_b = transposed(arrived_b, filt_a) + filt_b
        filt_a = jnp.where(usable, new_a, filt_a)
        filt_b = jnp.where(usable, new_b, filt_b)
        stored_q.append(smooth_q)
        smooth_q = jnp.where(segment + distance < segments, product(smooth_q, arrived_q), smooth_q)
    stored_q.append(smooth_q)
    top = 2**levels
    prefix = transposed(initial_mean, filt_a) + filt_b
    if top < segments:
        arrived = shifted(prefix, top, segments)
        prefix = jnp.where(segment >= top, transposed(arrived, filt_a) + filt_b, prefix)
    entry = jnp.where(segment == 0, initial_mean, shifted(prefix, 1, segments))
    filtered = []
    current = entry
    for j in range(span):
        current = transposed(current, transition) * scales[j][None, :] + pushes[j]
        filtered.append(current)
    filtered = jnp.stack(filtered)
    mapped = product(
        transposed(filtered.reshape(span * seq_total, state_width), transition), transition
    ).reshape(span, seq_total, state_width)
    gaps = filtered - keeps[:, None, None] * mapped * scales[:, None, :]
    offsets = jnp.zeros((seq_total, state_width), jnp.float32)
    for j in range(last, -1, -1):
        offsets = keeps[j] * product(offsets, transition) * scales[j][None, :] + gaps[j]
    for level in range(levels):
        distance = 2**level
        arrived = shifted(offsets, -distance, segments)
        offsets = jnp.where(
            segment + distance < segments, transposed(arrived, stored_q[level]) + offsets, offsets
        )
    if top < segments:
        arrived = shifted(offsets, -top, segments)
        offsets = jnp.where(
            segment + top < segments, transposed(arrived, stored_q[levels]) + offsets, offsets
        )
    current = shifted(offsets, -1, segments)
    smoothed = [None] * span
    for j in range(last, -1, -1):
        current = keeps[j] * product(current, transition) * scales[j][None, :] + gaps[j]
        smoothed[j] = current
    smoothed = jnp.stack(smoothed)
    both = jnp.stack([filtered, smoothed])
    both = lax.all_to_all(both, "state", split_axis=2, concat_axis=1, tiled=True)
    return (both[0], both[1])


def solution(mesh):
    return jax.shard_map(
        per_device,
        mesh=mesh,
        in_specs=(P("state", None), P(), P(), P("tm", None), P("tm"), P("tm")),
        out_specs=(P("tm", "state", None), P("tm", "state", None)),
        check_vma=False,
    )
```

profile of v0, /device:TPU:232, one launch (start us, length us, event | category | flops | bytes accessed | tf_op | source)
XLA Modules:
  0.0 522.6 jit_solution(9289157682158466495)
XLA Ops:
  9.4 27.4 %all-gather.2.cloned.1.call-done = f32[512,512]{1,0:T(8,128)} async-done(((f32[128,512]{1,0:T(8,128)}), f32[512,512]{1,0:T(8,128)}) %all-gather.2.cloned.1.call-update) | async-done | bytes 1048592 | tf_op jit(solution)/shard_map/all_gather | solution.py:51
  43.9 2.2 collective-permute-start
  46.2 20.8 %collective-permute-done = f32[512,512]{1,0:T(8,128)} collective-permute-done((f32[512,512]{1,0:T(8,128)S(1)}, f32[512,512]{1,0:T(8,128)}, u32[]{:S(2)}, u32[]{:S(2)}) %collective-permute-start) | collective-permute-done | bytes 1048608 | tf_op jit(solution)/shard_map/ppermute | solution.py:35
  67.0 3.1 convolution_select_fusion.13
  70.1 6.3 %collective-permute-start.1 = (f32[512,512]{1,0:T(8,128)S(1)}, f32[512,512]{1,0:T(8,128)}, u32[]{:S(2)}, u32[]{:S(2)}) collective-permute-start(f32[512,512]{1,0:T(8,128)S(1)} %convolution_select_fusion.13), channel_id=1, source_target_pairs={{0,2},{1,3},{2,4},{3,5},{4,6},{5,7},{6,8},{7,9},{8,10},{9,11},{10,... | collective-permute-start | bytes 3145736 | tf_op jit(solution)/shard_map/ppermute | solution.py:35
  77.1 22.1 %collective-permute-done.1 = f32[512,512]{1,0:T(8,128)} collective-permute-done((f32[512,512]{1,0:T(8,128)S(1)}, f32[512,512]{1,0:T(8,128)}, u32[]{:S(2)}, u32[]{:S(2)}) %collective-permute-start.1) | collective-permute-done | bytes 1048608 | tf_op jit(solution)/shard_map/ppermute | solution.py:35
  99.2 3.1 convolution_select_fusion.12
  102.3 2.7 collective-permute-start.2
  105.0 4.9 fusion.7
  109.9 2.5 fusion.6
  112.4 2.6 fusion.5
  115.0 3.1 collective-permute-start.18
  118.9 2.9 convolution_select_fusion.11
  121.8 4.9 collective-permute-start.3
  126.6 2.8 multiply_reduce_fusion
  129.5 13.0 %collective-permute-done.18 = f32[512,512]{1,0:T(8,128)} collective-permute-done((f32[512,512]{1,0:T(8,128)S(1)}, f32[512,512]{1,0:T(8,128)}, u32[]{:S(2)}, u32[]{:S(2)}) %collective-permute-start.18) | collective-permute-done | bytes 1048608 | tf_op jit(solution)/shard_map/ppermute | solution.py:35
  142.4 3.1 convolution_select_fusion.6
  145.5 6.5 %collective-permute-start.20 = (f32[512,512]{1,0:T(8,128)S(1)}, f32[512,512]{1,0:T(8,128)S(1)}, u32[]{:S(2)}, u32[]{:S(2)}) collective-permute-start(f32[512,512]{1,0:T(8,128)S(1)} %convolution_select_fusion.6), channel_id=1, source_target_pairs={{2,0},{3,1},{4,2},{5,3},{6,4},{7,5},{8,6},{9,7},{10,8},{11,9},{12,... | collective-permute-start | bytes 3145736 | tf_op jit(solution)/shard_map/ppermute | solution.py:35
  153.0 3.7 convolution_select_fusion.10
  156.8 3.3 collective-permute-start.4
  164.1 11.0 %collective-permute-done.20 = f32[512,512]{1,0:T(8,128)S(1)} collective-permute-done((f32[512,512]{1,0:T(8,128)S(1)}, f32[512,512]{1,0:T(8,128)S(1)}, u32[]{:S(2)}, u32[]{:S(2)}) %collective-permute-start.20) | collective-permute-done | bytes 1048608 | tf_op jit(solution)/shard_map/ppermute | solution.py:35
  175.1 2.9 convolution_select_fusion.5
  177.9 2.4 collective-permute-start.22
  180.3 21.0 %collective-permute-done.7 = f32[4,512]{1,0:T(4,128)S(1)} collective-permute-done((f32[4,512]{1,0:T(4,128)S(1)}, f32[4,512]{1,0:T(4,128)S(1)}, u32[]{:S(2)}, u32[]{:S(2)}) %collective-permute-start.7) | collective-permute-done | bytes 8224 | tf_op jit(solution)/shard_map/ppermute | solution.py:35
  204.3 2.8 collective-permute-done.4
  207.2 2.9 convolution_select_fusion.9
  210.0 9.3 %collective-permute-start.5 = (f32[512,512]{1,0:T(8,128)}, f32[512,512]{1,0:T(8,128)}, u32[]{:S(2)}, u32[]{:S(2)}) collective-permute-start(f32[512,512]{1,0:T(8,128)} %convolution_select_fusion.9), channel_id=1, source_target_pairs={{0,32},{1,33},{2,34},{3,35},{4,36},{5,37},{6,38},{7,39},{8,40},{9,... | collective-permute-start | bytes 3145736 | tf_op jit(solution)/shard_map/ppermute | solution.py:35
  222.3 11.1 %collective-permute-done.9 = f32[4,512]{1,0:T(4,128)S(1)} collective-permute-done((f32[4,512]{1,0:T(4,128)S(1)}, f32[4,512]{1,0:T(4,128)S(1)}, u32[]{:S(2)}, u32[]{:S(2)}) %collective-permute-start.9) | collective-permute-done | bytes 8224 | tf_op jit(solution)/shard_map/ppermute | solution.py:35
  233.4 2.2 fusion.43
  235.6 2.1 collective-permute-start.10
  237.7 4.7 convolution_select_fusion.4
  242.4 3.9 collective-permute-start.24
  246.3 14.5 %collective-permute-done.10 = f32[4,512]{1,0:T(4,128)S(1)} collective-permute-done((f32[4,512]{1,0:T(4,128)S(1)}, f32[4,512]{1,0:T(4,128)S(1)}, u32[]{:S(2)}, u32[]{:S(2)}) %collective-permute-start.10) | collective-permute-done | bytes 8224 | tf_op jit(solution)/shard_map/ppermute | solution.py:35
  260.8 2.2 fusion.42
  263.0 18.0 %collective-permute-start.11 = (f32[4,512]{1,0:T(4,128)S(1)}, f32[4,512]{1,0:T(4,128)S(1)}, u32[]{:S(2)}, u32[]{:S(2)}) collective-permute-start(f32[4,512]{1,0:T(4,128)S(1)} %fusion.42), channel_id=1, source_target_pairs={{0,16},{1,17},{2,18},{3,19},{4,20},{5,21},{6,22},{7,23},{8,24},{9,... | collective-permute-start | bytes 24584 | tf_op jit(solution)/shard_map/ppermute | solution.py:35
  281.0 4.7 convolution_select_fusion.8
  288.6 2.5 collective-permute-start.12
  291.1 6.9 %collective-permute-done.12 = f32[4,512]{1,0:T(4,128)S(1)} collective-permute-done((f32[4,512]{1,0:T(4,128)S(1)}, f32[4,512]{1,0:T(4,128)S(1)}, u32[]{:S(2)}, u32[]{:S(2)}) %collective-permute-start.12) | collective-permute-done | bytes 8224 | tf_op jit(solution)/shard_map/ppermute | solution.py:35
  298.0 2.2 fusion.40
  302.1 4.7 convolution_select_fusion.3
  306.8 4.8 collective-permute-start.26
  311.7 2.2 fusion.39
  313.9 3.7 convolution_select_fusion.7
  322.2 2.2 fusion.38
  324.4 4.4 collective-permute-start.15
  328.8 30.4 %collective-permute-done.26 = f32[512,512]{1,0:T(8,128)} collective-permute-done((f32[512,512]{1,0:T(8,128)}, f32[512,512]{1,0:T(8,128)}, u32[]{:S(2)}, u32[]{:S(2)}) %collective-permute-start.26) | collective-permute-done | bytes 1048608 | tf_op jit(solution)/shard_map/ppermute | solution.py:35
  359.3 4.7 convolution_select_fusion.2
  378.5 20.1 %collective-permute-done.16 = f32[4,512]{1,0:T(4,128)S(1)} collective-permute-done((f32[4,512]{1,0:T(4,128)S(1)}, f32[4,512]{1,0:T(4,128)S(1)}, u32[]{:S(2)}, u32[]{:S(2)}) %collective-permute-start.16) | collective-permute-done | bytes 8224 | tf_op jit(solution)/shard_map/ppermute | solution.py:35
  399.6 32.2 %collective-permute-start.17 = (f32[4,512]{1,0:T(4,128)S(1)}, f32[4,512]{1,0:T(4,128)S(1)}, u32[]{:S(2)}, u32[]{:S(2)}) collective-permute-start(f32[4,512]{1,0:T(4,128)S(1)} %fusion.24), channel_id=1, source_target_pairs={{2,0},{3,1},{4,2},{5,3},{6,4},{7,5},{8,6},{9,7},{10,8},{11,9},{12,... | collective-permute-start | bytes 24584 | tf_op jit(solution)/shard_map/ppermute | solution.py:35
  434.1 3.3 collective-permute-start.19
  437.5 3.7 convolution_select_fusion.1
  441.2 2.2 collective-permute-start.30
  443.4 2.2 fusion.22
  445.6 4.6 collective-permute-start.21
  450.2 3.1 collective-permute-done.21
  453.3 2.2 fusion.21
  457.4 6.7 %collective-permute-done.23 = f32[4,512]{1,0:T(4,128)S(1)} collective-permute-done((f32[4,512]{1,0:T(4,128)S(1)}, f32[4,512]{1,0:T(4,128)S(1)}, u32[]{:S(2)}, u32[]{:S(2)}) %collective-permute-start.23) | collective-permute-done | bytes 8224 | tf_op jit(solution)/shard_map/ppermute | solution.py:35
  464.2 2.2 fusion.20
  468.3 8.4 %collective-permute-done.25 = f32[4,512]{1,0:T(4,128)S(1)} collective-permute-done((f32[4,512]{1,0:T(4,128)S(1)}, f32[4,512]{1,0:T(4,128)S(1)}, u32[]{:S(2)}, u32[]{:S(2)}) %collective-permute-start.25) | collective-permute-done | bytes 8224 | tf_op jit(solution)/shard_map/ppermute | solution.py:35
  476.7 2.2 fusion.19
  480.8 3.6 collective-permute-done.27
  488.6 3.9 collective-permute-done.29
  495.3 3.6 collective-permute-done.31
  504.1 9.9 %all_to_all.15 = f32[2,4,4,512]{3,1,0,2:T(4,128)S(1)} all-to-all(f32[2,4,4,512]{3,1,0,2:T(4,128)S(1)} %copy.10), channel_id=1, replica_groups=mesh['tm'=64,'state'=4] {'state'}, dimensions={2} | all-to-all | bytes 131072 | tf_op jit(solution)/shard_map/all_to_all | solution.py:125
  (111 shorter events, 68.0 us)
Async XLA Ops:
  7.2 111.0 %copy-start = (f32[16,4]{0,1:T(4,128)S(1)}, f32[16,4]{0,1:T(4,128)}, u32[]{:S(2)}) copy-start(f32[16,4]{0,1:T(4,128)} %param.9) | copy-start | bytes 772
  7.2 29.6 %all-gather.2.cloned.1.call-start = ((), (), s32[]{:S(2)}) async-start(), calls=%async_computation.1 | async-start | bytes 1310720 | tf_op jit(solution)/shard_map/all_gather | solution.py:51
  7.9 0.8 copy-start.13
  7.9 0.7 copy-start.12
  8.6 0.7 copy-start.11
  36.8 1.2 copy-start.9
  43.9 26.1 %copy-start.7 = (f32[512,512]{1,0:T(8,128)}, f32[512,512]{1,0:T(8,128)S(1)}, u32[]{:S(2)}) copy-start(f32[512,512]{1,0:T(8,128)S(1)} %convolution_multiply_fusion.3) | copy-start | bytes 3145732
  43.9 23.0 %collective-permute-start = (f32[512,512]{1,0:T(8,128)S(1)}, f32[512,512]{1,0:T(8,128)}, u32[]{:S(2)}, u32[]{:S(2)}) collective-permute-start(f32[512,512]{1,0:T(8,128)S(1)} %convolution_multiply_fusion.3), channel_id=1, source_target_pairs={{0,1},{1,2},{2,3},{3,4},{4,5},{5,6},{6,7},{7,8},{8,9},{9,10},{10,1... | collective-permute-start | bytes 3145736 | tf_op jit(solution)/shard_map/ppermute | solution.py:35
  70.1 32.2 %copy-start.1 = (f32[512,512]{1,0:T(8,128)}, f32[512,512]{1,0:T(8,128)S(1)}, u32[]{:S(2)}) copy-start(f32[512,512]{1,0:T(8,128)S(1)} %convolution_select_fusion.13) | copy-start | bytes 3145732
  70.1 29.1 %collective-permute-start.1 = (f32[512,512]{1,0:T(8,128)S(1)}, f32[512,512]{1,0:T(8,128)}, u32[]{:S(2)}, u32[]{:S(2)}) collective-permute-start(f32[512,512]{1,0:T(8,128)S(1)} %convolution_select_fusion.13), channel_id=1, source_target_pairs={{0,2},{1,3},{2,4},{3,5},{4,6},{5,7},{6,8},{7,9},{8,10},{9,11},{10,... | collective-permute-start | bytes 3145736 | tf_op jit(solution)/shard_map/ppermute | solution.py:35
  102.3 16.6 %copy-start.3 = (f32[512,512]{1,0:T(8,128)}, f32[512,512]{1,0:T(8,128)S(1)}, u32[]{:S(2)}) copy-start(f32[512,512]{1,0:T(8,128)S(1)} %convolution_select_fusion.12) | copy-start | bytes 3145732
  102.3 16.6 %collective-permute-start.2 = (f32[512,512]{1,0:T(8,128)S(1)}, f32[512,512]{1,0:T(8,128)S(1)}, u32[]{:S(2)}, u32[]{:S(2)}) collective-permute-start(f32[512,512]{1,0:T(8,128)S(1)} %convolution_select_fusion.12), channel_id=1, source_target_pairs={{0,4},{1,5},{2,6},{3,7},{4,8},{5,9},{6,10},{7,11},{8,12},{9,13},{1... | collective-permute-start | bytes 3145736 | tf_op jit(solution)/shard_map/ppermute | solution.py:35
  115.0 27.5 %collective-permute-start.18 = (f32[512,512]{1,0:T(8,128)S(1)}, f32[512,512]{1,0:T(8,128)}, u32[]{:S(2)}, u32[]{:S(2)}) collective-permute-start(f32[512,512]{1,0:T(8,128)S(1)} %fusion.5), channel_id=1, source_target_pairs={{1,0},{2,1},{3,2},{4,3},{5,4},{6,5},{7,6},{8,7},{9,8},{10,9},{11,1... | collective-permute-start | bytes 3145736 | tf_op jit(solution)/shard_map/ppermute | solution.py:35
  121.8 31.3 %collective-permute-start.3 = (f32[512,512]{1,0:T(8,128)}, f32[512,512]{1,0:T(8,128)}, u32[]{:S(2)}, u32[]{:S(2)}) collective-permute-start(f32[512,512]{1,0:T(8,128)} %convolution_select_fusion.11), channel_id=1, source_target_pairs={{0,8},{1,9},{2,10},{3,11},{4,12},{5,13},{6,14},{7,15},{8,16},{9,17... | collective-permute-start | bytes 3145736 | tf_op jit(solution)/shard_map/ppermute | solution.py:35
  145.5 29.5 %collective-permute-start.20 = (f32[512,512]{1,0:T(8,128)S(1)}, f32[512,512]{1,0:T(8,128)S(1)}, u32[]{:S(2)}, u32[]{:S(2)}) collective-permute-start(f32[512,512]{1,0:T(8,128)S(1)} %convolution_select_fusion.6), channel_id=1, source_target_pairs={{2,0},{3,1},{4,2},{5,3},{6,4},{7,5},{8,6},{9,7},{10,8},{11,9},{12,... | collective-permute-start | bytes 3145736 | tf_op jit(solution)/shard_map/ppermute | solution.py:35
  156.8 50.4 %copy-start.4 = (f32[512,512]{1,0:T(8,128)}, f32[512,512]{1,0:T(8,128)S(1)}, u32[]{:S(2)}) copy-start(f32[512,512]{1,0:T(8,128)S(1)} %convolution_select_fusion.10) | copy-start | bytes 3145732
  156.8 50.4 %collective-permute-start.4 = (f32[512,512]{1,0:T(8,128)S(1)}, f32[512,512]{1,0:T(8,128)S(1)}, u32[]{:S(2)}, u32[]{:S(2)}) collective-permute-start(f32[512,512]{1,0:T(8,128)S(1)} %convolution_select_fusion.10), channel_id=1, source_target_pairs={{0,16},{1,17},{2,18},{3,19},{4,20},{5,21},{6,22},{7,23},{8,24},{9,... | collective-permute-start | bytes 3145736 | tf_op jit(solution)/shard_map/ppermute | solution.py:35
  162.0 39.3 %copy-start.8 = (f32[512,512]{1,0:T(8,128)S(1)}, f32[512,512]{1,0:T(8,128)}, u32[]{:S(2)}) copy-start(f32[512,512]{1,0:T(8,128)} %copy-done.7) | copy-start | bytes 3145732
  162.0 39.3 %collective-permute-start.7 = (f32[4,512]{1,0:T(4,128)S(1)}, f32[4,512]{1,0:T(4,128)S(1)}, u32[]{:S(2)}, u32[]{:S(2)}) collective-permute-start(f32[4,512]{1,0:T(4,128)S(1)} %fusion.46), channel_id=1, source_target_pairs={{0,1},{1,2},{2,3},{3,4},{4,5},{5,6},{6,7},{7,8},{8,9},{9,10},{10,1... | collective-permute-start | bytes 24584 | tf_op jit(solution)/shard_map/ppermute | solution.py:35
  177.9 59.8 %collective-permute-start.22 = (f32[512,512]{1,0:T(8,128)}, f32[512,512]{1,0:T(8,128)}, u32[]{:S(2)}, u32[]{:S(2)}) collective-permute-start(f32[512,512]{1,0:T(8,128)} %convolution_select_fusion.5), channel_id=1, source_target_pairs={{4,0},{5,1},{6,2},{7,3},{8,4},{9,5},{10,6},{11,7},{12,8},{13,9},{1... | collective-permute-start | bytes 3145736 | tf_op jit(solution)/shard_map/ppermute | solution.py:35
  202.3 17.1 %copy-start.2 = (f32[512,512]{1,0:T(8,128)S(1)}, f32[512,512]{1,0:T(8,128)}, u32[]{:S(2)}) copy-start(f32[512,512]{1,0:T(8,128)} %copy-done.1) | copy-start | bytes 3145732
  202.3 17.1 %collective-permute-start.8 = (f32[4,512]{1,0:T(4,128)S(1)}, f32[4,512]{1,0:T(4,128)S(1)}, u32[]{:S(2)}, u32[]{:S(2)}) collective-permute-start(f32[4,512]{1,0:T(4,128)S(1)} %fusion.45), channel_id=1, source_target_pairs={{0,2},{1,3},{2,4},{3,5},{4,6},{5,7},{6,8},{7,9},{8,10},{9,11},{10,... | collective-permute-start | bytes 24584 | tf_op jit(solution)/shard_map/ppermute | solution.py:35
  210.0 70.9 %collective-permute-start.5 = (f32[512,512]{1,0:T(8,128)}, f32[512,512]{1,0:T(8,128)}, u32[]{:S(2)}, u32[]{:S(2)}) collective-permute-start(f32[512,512]{1,0:T(8,128)} %convolution_select_fusion.9), channel_id=1, source_target_pairs={{0,32},{1,33},{2,34},{3,35},{4,36},{5,37},{6,38},{7,39},{8,40},{9,... | collective-permute-start | bytes 3145736 | tf_op jit(solution)/shard_map/ppermute | solution.py:35
  220.4 13.0 %collective-permute-start.9 = (f32[4,512]{1,0:T(4,128)S(1)}, f32[4,512]{1,0:T(4,128)S(1)}, u32[]{:S(2)}, u32[]{:S(2)}) collective-permute-start(f32[4,512]{1,0:T(4,128)S(1)} %fusion.44), channel_id=1, source_target_pairs={{0,4},{1,5},{2,6},{3,7},{4,8},{5,9},{6,10},{7,11},{8,12},{9,13},{1... | collective-permute-start | bytes 24584 | tf_op jit(solution)/shard_map/ppermute | solution.py:35
  235.6 25.2 %collective-permute-start.10 = (f32[4,512]{1,0:T(4,128)S(1)}, f32[4,512]{1,0:T(4,128)S(1)}, u32[]{:S(2)}, u32[]{:S(2)}) collective-permute-start(f32[4,512]{1,0:T(4,128)S(1)} %fusion.43), channel_id=1, source_target_pairs={{0,8},{1,9},{2,10},{3,11},{4,12},{5,13},{6,14},{7,15},{8,16},{9,17... | collective-permute-start | bytes 24584 | tf_op jit(solution)/shard_map/ppermute | solution.py:35
  242.4 59.8 %collective-permute-start.24 = (f32[512,512]{1,0:T(8,128)}, f32[512,512]{1,0:T(8,128)}, u32[]{:S(2)}, u32[]{:S(2)}) collective-permute-start(f32[512,512]{1,0:T(8,128)} %convolution_select_fusion.4), channel_id=1, source_target_pairs={{8,0},{9,1},{10,2},{11,3},{12,4},{13,5},{14,6},{15,7},{16,8},{17,9... | collective-permute-start | bytes 3145736 | tf_op jit(solution)/shard_map/ppermute | solution.py:35
  262.9 24.6 %copy-start.5 = (f32[512,512]{1,0:T(8,128)S(1)}, f32[512,512]{1,0:T(8,128)}, u32[]{:S(2)}) copy-start(f32[512,512]{1,0:T(8,128)} %copy-done.4) | copy-start | bytes 3145732
  263.0 24.6 %collective-permute-start.11 = (f32[4,512]{1,0:T(4,128)S(1)}, f32[4,512]{1,0:T(4,128)S(1)}, u32[]{:S(2)}, u32[]{:S(2)}) collective-permute-start(f32[4,512]{1,0:T(4,128)S(1)} %fusion.42), channel_id=1, source_target_pairs={{0,16},{1,17},{2,18},{3,19},{4,20},{5,21},{6,22},{7,23},{8,24},{9,... | collective-permute-start | bytes 24584 | tf_op jit(solution)/shard_map/ppermute | solution.py:35
  285.7 28.2 %collective-permute-start.6 = (f32[512,512]{1,0:T(8,128)}, f32[512,512]{1,0:T(8,128)}, u32[]{:S(2)}, u32[]{:S(2)}) collective-permute-start(f32[512,512]{1,0:T(8,128)} %convolution_select_fusion.8), channel_id=1, source_target_pairs={{0,64},{1,65},{2,66},{3,67},{4,68},{5,69},{6,70},{7,71},{8,72},{9,... | collective-permute-start | bytes 3145736 | tf_op jit(solution)/shard_map/ppermute | solution.py:35
  288.6 9.5 %collective-permute-start.12 = (f32[4,512]{1,0:T(4,128)S(1)}, f32[4,512]{1,0:T(4,128)S(1)}, u32[]{:S(2)}, u32[]{:S(2)}) collective-permute-start(f32[4,512]{1,0:T(4,128)S(1)} %fusion.41), channel_id=1, source_target_pairs={{0,32},{1,33},{2,34},{3,35},{4,36},{5,37},{6,38},{7,39},{8,40},{9,... | collective-permute-start | bytes 24584 | tf_op jit(solution)/shard_map/ppermute | solution.py:35
  300.2 11.5 %collective-permute-start.13 = (f32[4,512]{1,0:T(4,128)S(1)}, f32[4,512]{1,0:T(4,128)S(1)}, u32[]{:S(2)}, u32[]{:S(2)}) collective-permute-start(f32[4,512]{1,0:T(4,128)S(1)} %fusion.40), channel_id=1, source_target_pairs={{0,64},{1,65},{2,66},{3,67},{4,68},{5,69},{6,70},{7,71},{8,72},{9,... | collective-permute-start | bytes 24584 | tf_op jit(solution)/shard_map/ppermute | solution.py:35
  306.8 52.4 %collective-permute-start.26 = (f32[512,512]{1,0:T(8,128)}, f32[512,512]{1,0:T(8,128)}, u32[]{:S(2)}, u32[]{:S(2)}) collective-permute-start(f32[512,512]{1,0:T(8,128)} %convolution_select_fusion.3), channel_id=1, source_target_pairs={{16,0},{17,1},{18,2},{19,3},{20,4},{21,5},{22,6},{23,7},{24,8},{25... | collective-permute-start | bytes 3145736 | tf_op jit(solution)/shard_map/ppermute | solution.py:35
  313.9 4.7 copy-start.10
  317.6 1.0 copy-start.6
  319.6 2.7 collective-permute-start.14
  324.4 41.5 %collective-permute-start.15 = (f32[4,512]{1,0:T(4,128)S(1)}, f32[4,512]{1,0:T(4,128)S(1)}, u32[]{:S(2)}, u32[]{:S(2)}) collective-permute-start(f32[4,512]{1,0:T(4,128)S(1)} %fusion.38), channel_id=1, source_target_pairs={{0,1},{1,2},{2,3},{3,4},{4,5},{5,6},{6,7},{7,8},{8,9},{9,10},{10,1... | collective-permute-start | bytes 24584 | tf_op jit(solution)/shard_map/ppermute | solution.py:35
  364.0 73.5 %collective-permute-start.28 = (f32[512,512]{1,0:T(8,128)}, f32[512,512]{1,0:T(8,128)}, u32[]{:S(2)}, u32[]{:S(2)}) collective-permute-start(f32[512,512]{1,0:T(8,128)} %convolution_select_fusion.2), channel_id=1, source_target_pairs={{32,0},{33,1},{34,2},{35,3},{36,4},{37,5},{38,6},{39,7},{40,8},{41... | collective-permute-start | bytes 3145736 | tf_op jit(solution)/shard_map/ppermute | solution.py:35
  376.6 22.0 %collective-permute-start.16 = (f32[4,512]{1,0:T(4,128)S(1)}, f32[4,512]{1,0:T(4,128)S(1)}, u32[]{:S(2)}, u32[]{:S(2)}) collective-permute-start(f32[4,512]{1,0:T(4,128)S(1)} %fusion.26), channel_id=1, source_target_pairs={{1,0},{2,1},{3,2},{4,3},{5,4},{6,5},{7,6},{8,7},{9,8},{10,9},{11,1... | collective-permute-start | bytes 24584 | tf_op jit(solution)/shard_map/ppermute | solution.py:35
  399.6 33.6 %collective-permute-start.17 = (f32[4,512]{1,0:T(4,128)S(1)}, f32[4,512]{1,0:T(4,128)S(1)}, u32[]{:S(2)}, u32[]{:S(2)}) collective-permute-start(f32[4,512]{1,0:T(4,128)S(1)} %fusion.24), channel_id=1, source_target_pairs={{2,0},{3,1},{4,2},{5,3},{6,4},{7,5},{8,6},{9,7},{10,8},{11,9},{12,... | collective-permute-start | bytes 24584 | tf_op jit(solution)/shard_map/ppermute | solution.py:35
  434.1 9.2 %collective-permute-start.19 = (f32[4,512]{1,0:T(4,128)S(1)}, f32[4,512]{1,0:T(4,128)S(1)}, u32[]{:S(2)}, u32[]{:S(2)}) collective-permute-start(f32[4,512]{1,0:T(4,128)S(1)} %fusion.23), channel_id=1, source_target_pairs={{4,0},{5,1},{6,2},{7,3},{8,4},{9,5},{10,6},{11,7},{12,8},{13,9},{1... | collective-permute-start | bytes 24584 | tf_op jit(solution)/shard_map/ppermute | solution.py:35
  441.2 45.5 %collective-permute-start.30 = (f32[512,512]{1,0:T(8,128)S(1)}, f32[512,512]{1,0:T(8,128)S(1)}, u32[]{:S(2)}, u32[]{:S(2)}) collective-permute-start(f32[512,512]{1,0:T(8,128)S(1)} %convolution_select_fusion.1), channel_id=1, source_target_pairs={{64,0},{65,1},{66,2},{67,3},{68,4},{69,5},{70,6},{71,7},{72,8},{73... | collective-permute-start | bytes 3145736 | tf_op jit(solution)/shard_map/ppermute | solution.py:35
  445.6 7.8 %collective-permute-start.21 = (f32[4,512]{1,0:T(4,128)S(1)}, f32[4,512]{1,0:T(4,128)S(1)}, u32[]{:S(2)}, u32[]{:S(2)}) collective-permute-start(f32[4,512]{1,0:T(4,128)S(1)} %fusion.22), channel_id=1, source_target_pairs={{8,0},{9,1},{10,2},{11,3},{12,4},{13,5},{14,6},{15,7},{16,8},{17,9... | collective-permute-start | bytes 24584 | tf_op jit(solution)/shard_map/ppermute | solution.py:35
  455.5 8.7 %collective-permute-start.23 = (f32[4,512]{1,0:T(4,128)S(1)}, f32[4,512]{1,0:T(4,128)S(1)}, u32[]{:S(2)}, u32[]{:S(2)}) collective-permute-start(f32[4,512]{1,0:T(4,128)S(1)} %fusion.21), channel_id=1, source_target_pairs={{16,0},{17,1},{18,2},{19,3},{20,4},{21,5},{22,6},{23,7},{24,8},{25... | collective-permute-start | bytes 24584 | tf_op jit(solution)/shard_map/ppermute | solution.py:35
  466.4 10.4 %collective-permute-start.25 = (f32[4,512]{1,0:T(4,128)S(1)}, f32[4,512]{1,0:T(4,128)S(1)}, u32[]{:S(2)}, u32[]{:S(2)}) collective-permute-start(f32[4,512]{1,0:T(4,128)S(1)} %fusion.20), channel_id=1, source_target_pairs={{32,0},{33,1},{34,2},{35,3},{36,4},{37,5},{38,6},{39,7},{40,8},{41... | collective-permute-start | bytes 24584 | tf_op jit(solution)/shard_map/ppermute | solution.py:35
  478.9 5.5 %collective-permute-start.27 = (f32[4,512]{1,0:T(4,128)S(1)}, f32[4,512]{1,0:T(4,128)S(1)}, u32[]{:S(2)}, u32[]{:S(2)}) collective-permute-start(f32[4,512]{1,0:T(4,128)S(1)} %fusion.19), channel_id=1, source_target_pairs={{64,0},{65,1},{66,2},{67,3},{68,4},{69,5},{70,6},{71,7},{72,8},{73... | collective-permute-start | bytes 24584 | tf_op jit(solution)/shard_map/ppermute | solution.py:35
  485.4 7.1 %collective-permute-start.29 = (f32[4,512]{1,0:T(4,128)S(1)}, f32[4,512]{1,0:T(4,128)S(1)}, u32[]{:S(2)}, u32[]{:S(2)}) collective-permute-start(f32[4,512]{1,0:T(4,128)S(1)} %fusion.18), channel_id=1, source_target_pairs={{128,0},{129,1},{130,2},{131,3},{132,4},{133,5},{134,6},{135,7},{1... | collective-permute-start | bytes 24584 | tf_op jit(solution)/shard_map/ppermute | solution.py:35
  493.4 5.5 %collective-permute-start.31 = (f32[4,512]{1,0:T(4,128)S(1)}, f32[4,512]{1,0:T(4,128)S(1)}, u32[]{:S(2)}, u32[]{:S(2)}) collective-permute-start(f32[4,512]{1,0:T(4,128)S(1)} %fusion.17), channel_id=1, source_target_pairs={{1,0},{2,1},{3,2},{4,3},{5,4},{6,5},{7,6},{8,7},{9,8},{10,9},{11,1... | collective-permute-start | bytes 24584 | tf_op jit(solution)/shard_map/ppermute | solution.py:35
Sparse Core Ops, SparseCore 0:
  9.8 26.9 all-gather.1
where the time goes:
time: 532 us; the launch traced here: 523 us
  waiting for transfers between devices  234 us (44%)
  starting transfers between devices  143 us (27%)
  matrix products  111 us (21%)
  between operations  15.2 us (3%)
  blocking collectives  9.88 us (2%)
  local copies, waits for them, and re-layouts  6.3 us (1%)
    ppermute x32, waiting for transfers between devices, shifted(): return lax.ppermute(block, AXES, route)  206 us
    ppermute x32, starting transfers between devices, shifted(): return lax.ppermute(block, AXES, route)  143 us
    dot_general x26, matrix products, product(): jnp.dot(left, right, precision=lax.Precision.HIGHEST, preferred_element_t...  66.1 us
    dot_general x25, matrix products, transposed(): lax.dot_general(left, right, (((1,), (1,)), ((), ())), precision=lax.Prec...  35.1 us
    all_gather x1, waiting for transfers between devices, per_device(): lax.all_gather(dynamics, 'state', axis=0, tiled=True) * block_mask  27.4 us
  transfers between devices with their start and end apart: 33, of which 20 were waited for; matrix products, arithmetic and copies ran while one was open for 19% of the time, Pallas kernels for 0%

commit v1 on v0

--- a/solution.py
+++ b/solution.py
@@ -48,7 +48,16 @@
     steps_total = span * segments
     present = jnp.maximum(pattern, jnp.eye(blocks, dtype=jnp.int32))
     block_mask = jnp.repeat(jnp.repeat(present, block_span, 0), block_span, 1).astype(jnp.float32)
-    transition = lax.all_gather(dynamics, "state", axis=0, tiled=True) * block_mask
+    trace_lots_all_by_axis = lambda mine, d_out: jnp.concatenate(
+        lax.all_to_all(
+            jnp.stack(lax.axis_size("state") * [mine], axis=0),
+            concat_axis=0,
+            axis_name="state",
+            split_axis=0,
+        ),
+        d_out,
+    )
+    transition = trace_lots_all_by_axis(dynamics, 0) * block_mask
     first = member * span
     obs_here = lax.dynamic_slice_in_dim(observed, first, span, 0)
     index_here = lax.dynamic_slice_in_dim(obs_index, first, span, 0)

time: 532 us -> 514 us (0.966)
  the two profiles are of different devices: /device:TPU:232 before, /device:TPU:72 now
where the time goes in v1:
time: 514 us; the launch traced here: 504 us
  starting transfers between devices  186 us (36%)
  waiting for transfers between devices  179 us (35%)
  matrix products  112 us (22%)
  local copies, waits for them, and re-layouts  9.96 us (2%)
  blocking collectives  9.75 us (2%)
  other arithmetic  5.15 us (1%)
    ppermute x32, starting transfers between devices, shifted(): return lax.ppermute(block, AXES, route)  182 us
    ppermute x32, waiting for transfers between devices, shifted(): return lax.ppermute(block, AXES, route)  168 us
    dot_general x26, matrix products, product(): jnp.dot(left, right, precision=lax.Precision.HIGHEST, preferred_element_t...  66.9 us
    dot_general x25, matrix products, transposed(): lax.dot_general(left, right, (((1,), (1,)), ((), ())), precision=lax.Prec...  35.1 us
    all_to_all x1, waiting for transfers between devices, per_device(): lax.all_to_all(jnp.stack(lax.axis_size('state') * [mine], axis=0), concat...  10.9 us
  transfers between devices with their start and end apart: 33, of which 18 were waited for; matrix products, arithmetic and copies ran while one was open for 20% of the time, Pallas kernels for 0%

profile of v1, /device:TPU:72, one launch (start us, length us, event | category | flops | bytes accessed | tf_op | source)
XLA Modules:
  0.0 503.9 jit_solution(7206248354455469568)
XLA Ops:
  2.7 4.3 all-to-all-start
  11.2 10.9 %all-to-all-done = f32[4,128,512]{2,1,0:T(8,128)S(1)} async-done(((f32[4,128,512]{2,1,0:T(8,128)}), f32[4,128,512]{2,1,0:T(8,128)S(1)}, u32[]{:S(2)}, u32[]{:S(2)}) %all-to-all-start) | async-done | bytes 1048608 | tf_op jit(solution)/shard_map/all_to_all | solution.py:52
  29.8 2.5 collective-permute-start
  32.3 21.2 %collective-permute-done = f32[512,512]{1,0:T(8,128)} collective-permute-done((f32[512,512]{1,0:T(8,128)S(1)}, f32[512,512]{1,0:T(8,128)}, u32[]{:S(2)}, u32[]{:S(2)}) %collective-permute-start) | collective-permute-done | bytes 1048608 | tf_op jit(solution)/shard_map/ppermute | solution.py:35
  53.5 3.7 convolution_select_fusion.13
  57.3 4.8 collective-permute-start.1
  62.8 22.8 %collective-permute-done.1 = f32[512,512]{1,0:T(8,128)} collective-permute-done((f32[512,512]{1,0:T(8,128)S(1)}, f32[512,512]{1,0:T(8,128)}, u32[]{:S(2)}, u32[]{:S(2)}) %collective-permute-start.1) | collective-permute-done | bytes 1048608 | tf_op jit(solution)/shard_map/ppermute | solution.py:35
  85.6 3.1 convolution_select_fusion.12
  88.7 3.5 collective-permute-start.2
  92.2 4.8 fusion.2
  97.0 2.5 fusion.1
  99.6 2.6 fusion
  102.2 3.0 collective-permute-start.18
  105.9 2.9 convolution_select_fusion.11
  108.8 3.8 collective-permute-start.3
  112.6 2.8 multiply_reduce_fusion
  115.6 14.3 %collective-permute-done.18 = f32[512,512]{1,0:T(8,128)} collective-permute-done((f32[512,512]{1,0:T(8,128)S(1)}, f32[512,512]{1,0:T(8,128)}, u32[]{:S(2)}, u32[]{:S(2)}) %collective-permute-start.18) | collective-permute-done | bytes 1048608 | tf_op jit(solution)/shard_map/ppermute | solution.py:35
  129.9 3.1 convolution_select_fusion.6
  133.0 4.7 collective-permute-start.20
  138.7 3.7 convolution_select_fusion.10
  142.4 6.4 %collective-permute-start.4 = (f32[512,512]{1,0:T(8,128)S(1)}, f32[512,512]{1,0:T(8,128)S(1)}, u32[]{:S(2)}, u32[]{:S(2)}) collective-permute-start(f32[512,512]{1,0:T(8,128)S(1)} %convolution_select_fusion.10), channel_id=1, source_target_pairs={{0,16},{1,17},{2,18},{3,19},{4,20},{5,21},{6,22},{7,23},{8,24},{9,... | collective-permute-start | bytes 3145736 | tf_op jit(solution)/shard_map/ppermute | solution.py:35
  150.8 2.5 collective-permute-start.7
  153.3 8.3 %collective-permute-done.20 = f32[512,512]{1,0:T(8,128)S(1)} collective-permute-done((f32[512,512]{1,0:T(8,128)S(1)}, f32[512,512]{1,0:T(8,128)S(1)}, u32[]{:S(2)}, u32[]{:S(2)}) %collective-permute-start.20) | collective-permute-done | bytes 1048608 | tf_op jit(solution)/shard_map/ppermute | solution.py:35
  161.6 2.9 convolution_select_fusion.5
  166.4 27.6 %collective-permute-done.7 = f32[4,512]{1,0:T(4,128)S(1)} collective-permute-done((f32[4,512]{1,0:T(4,128)S(1)}, f32[4,512]{1,0:T(4,128)S(1)}, u32[]{:S(2)}, u32[]{:S(2)}) %collective-permute-start.7) | collective-permute-done | bytes 8224 | tf_op jit(solution)/shard_map/ppermute | solution.py:35
  197.1 2.9 convolution_select_fusion.9
  200.0 3.7 collective-permute-start.5
  206.7 3.8 collective-permute-done.9
  210.5 2.2 fusion.40
  212.7 22.1 %collective-permute-start.10 = (f32[4,512]{1,0:T(4,128)S(1)}, f32[4,512]{1,0:T(4,128)S(1)}, u32[]{:S(2)}, u32[]{:S(2)}) collective-permute-start(f32[4,512]{1,0:T(4,128)S(1)} %fusion.40), channel_id=1, source_target_pairs={{0,8},{1,9},{2,10},{3,11},{4,12},{5,13},{6,14},{7,15},{8,16},{9,17... | collective-permute-start | bytes 24584 | tf_op jit(solution)/shard_map/ppermute | solution.py:35
  234.8 4.7 convolution_select_fusion.4
  239.5 23.4 %collective-permute-start.24 = (f32[512,512]{1,0:T(8,128)}, f32[512,512]{1,0:T(8,128)}, u32[]{:S(2)}, u32[]{:S(2)}) collective-permute-start(f32[512,512]{1,0:T(8,128)} %convolution_select_fusion.4), channel_id=1, source_target_pairs={{8,0},{9,1},{10,2},{11,3},{12,4},{13,5},{14,6},{15,7},{16,8},{17,9... | collective-permute-start | bytes 3145736 | tf_op jit(solution)/shard_map/ppermute | solution.py:35
  262.9 2.2 fusion.39
  265.1 2.9 collective-permute-start.11
  268.0 4.8 convolution_select_fusion.8
  272.8 3.4 collective-permute-start.6
  277.2 5.3 %collective-permute-start.12 = (f32[4,512]{1,0:T(4,128)S(1)}, f32[4,512]{1,0:T(4,128)S(1)}, u32[]{:S(2)}, u32[]{:S(2)}) collective-permute-start(f32[4,512]{1,0:T(4,128)S(1)} %fusion.38), channel_id=1, source_target_pairs={{0,32},{1,33},{2,34},{3,35},{4,36},{5,37},{6,38},{7,39},{8,40},{9,... | collective-permute-start | bytes 24584 | tf_op jit(solution)/shard_map/ppermute | solution.py:35
  282.6 5.1 %collective-permute-done.12 = f32[4,512]{1,0:T(4,128)S(1)} collective-permute-done((f32[4,512]{1,0:T(4,128)S(1)}, f32[4,512]{1,0:T(4,128)S(1)}, u32[]{:S(2)}, u32[]{:S(2)}) %collective-permute-start.12) | collective-permute-done | bytes 8224 | tf_op jit(solution)/shard_map/ppermute | solution.py:35
  287.7 2.2 fusion.37
  291.8 4.7 convolution_select_fusion.3
  296.5 3.8 collective-permute-start.26
  300.3 2.2 fusion.36
  302.5 3.7 convolution_select_fusion.7
  308.3 3.2 collective-permute-start.14
  312.8 2.2 fusion.35
  317.1 28.6 %collective-permute-done.26 = f32[512,512]{1,0:T(8,128)} collective-permute-done((f32[512,512]{1,0:T(8,128)}, f32[512,512]{1,0:T(8,128)}, u32[]{:S(2)}, u32[]{:S(2)}) %collective-permute-start.26) | collective-permute-done | bytes 1048608 | tf_op jit(solution)/shard_map/ppermute | solution.py:35
  345.8 4.8 convolution_select_fusion.2
  350.5 52.2 %collective-permute-start.28 = (f32[512,512]{1,0:T(8,128)}, f32[512,512]{1,0:T(8,128)}, u32[]{:S(2)}, u32[]{:S(2)}) collective-permute-start(f32[512,512]{1,0:T(8,128)} %convolution_select_fusion.2), channel_id=1, source_target_pairs={{32,0},{33,1},{34,2},{35,3},{36,4},{37,5},{38,6},{39,7},{40,8},{41... | collective-permute-start | bytes 3145736 | tf_op jit(solution)/shard_map/ppermute | solution.py:35
  415.3 3.6 collective-permute-done.16
  421.8 5.1 %collective-permute-done.17 = f32[4,512]{1,0:T(4,128)S(1)} collective-permute-done((f32[4,512]{1,0:T(4,128)S(1)}, f32[4,512]{1,0:T(4,128)S(1)}, u32[]{:S(2)}, u32[]{:S(2)}) %collective-permute-start.17) | collective-permute-done | bytes 8224 | tf_op jit(solution)/shard_map/ppermute | solution.py:35
  429.9 3.7 convolution_select_fusion.1
  433.6 2.2 collective-permute-start.30
  435.8 2.2 fusion.19
  439.9 3.6 collective-permute-done.21
  443.5 2.2 fusion.18
  447.6 5.7 %collective-permute-done.23 = f32[4,512]{1,0:T(4,128)S(1)} collective-permute-done((f32[4,512]{1,0:T(4,128)S(1)}, f32[4,512]{1,0:T(4,128)S(1)}, u32[]{:S(2)}, u32[]{:S(2)}) %collective-permute-start.23) | collective-permute-done | bytes 8224 | tf_op jit(solution)/shard_map/ppermute | solution.py:35
  453.4 2.2 fusion.17
  455.6 3.9 collective-permute-start.25
  459.4 5.6 %collective-permute-done.25 = f32[4,512]{1,0:T(4,128)S(1)} collective-permute-done((f32[4,512]{1,0:T(4,128)S(1)}, f32[4,512]{1,0:T(4,128)S(1)}, u32[]{:S(2)}, u32[]{:S(2)}) %collective-permute-start.25) | collective-permute-done | bytes 8224 | tf_op jit(solution)/shard_map/ppermute | solution.py:35
  465.0 2.2 fusion.16
  469.1 3.6 collective-permute-done.27
  476.9 3.9 collective-permute-done.29
  483.7 3.6 collective-permute-done.31
  492.4 9.8 %all_to_all.20 = f32[2,4,4,512]{3,1,0,2:T(4,128)S(1)} all-to-all(f32[2,4,4,512]{3,1,0,2:T(4,128)S(1)} %copy.10), channel_id=1, replica_groups=mesh['tm'=64,'state'=4] {'state'}, dimensions={2} | all-to-all | bytes 131072 | tf_op jit(solution)/shard_map/all_to_all | solution.py:134
  (116 shorter events, 72.1 us)
Async XLA Ops:
  0.6 104.5 %copy-start = (f32[16,4]{0,1:T(4,128)S(1)}, f32[16,4]{0,1:T(4,128)}, u32[]{:S(2)}) copy-start(f32[16,4]{0,1:T(4,128)} %param.9) | copy-start | bytes 772
  2.7 19.4 %all-to-all-start = ((f32[4,128,512]{2,1,0:T(8,128)}), f32[4,128,512]{2,1,0:T(8,128)S(1)}, u32[]{:S(2)}, u32[]{:S(2)}) async-start(f32[4,128,512]{2,1,0:T(8,128)} %stack.46), calls=%async_computation | async-start | bytes 2097152 | tf_op jit(solution)/shard_map/all_to_all | solution.py:52
  7.0 0.7 copy-start.14
  9.8 0.7 copy-start.15
  10.4 0.7 copy-start.16
  22.1 1.8 copy-start.8
  23.9 1.9 copy-start.9
  29.8 2.5 copy-start.11
  29.8 23.7 %collective-permute-start = (f32[512,512]{1,0:T(8,128)S(1)}, f32[512,512]{1,0:T(8,128)}, u32[]{:S(2)}, u32[]{:S(2)}) collective-permute-start(f32[512,512]{1,0:T(8,128)S(1)} %convolution_multiply_fusion.3), channel_id=1, source_target_pairs={{0,1},{1,2},{2,3},{3,4},{4,5},{5,6},{6,7},{7,8},{8,9},{9,10},{10,1... | collective-permute-start | bytes 3145736 | tf_op jit(solution)/shard_map/ppermute | solution.py:35
  57.3 31.4 %copy-start.3 = (f32[512,512]{1,0:T(8,128)}, f32[512,512]{1,0:T(8,128)S(1)}, u32[]{:S(2)}) copy-start(f32[512,512]{1,0:T(8,128)S(1)} %convolution_select_fusion.13) | copy-start | bytes 3145732
  57.3 28.3 %collective-permute-start.1 = (f32[512,512]{1,0:T(8,128)S(1)}, f32[512,512]{1,0:T(8,128)}, u32[]{:S(2)}, u32[]{:S(2)}) collective-permute-start(f32[512,512]{1,0:T(8,128)S(1)} %convolution_select_fusion.13), channel_id=1, source_target_pairs={{0,2},{1,3},{2,4},{3,5},{4,6},{5,7},{6,8},{7,9},{8,10},{9,11},{10,... | collective-permute-start | bytes 3145736 | tf_op jit(solution)/shard_map/ppermute | solution.py:35
  88.7 17.2 %copy-start.5 = (f32[512,512]{1,0:T(8,128)}, f32[512,512]{1,0:T(8,128)S(1)}, u32[]{:S(2)}) copy-start(f32[512,512]{1,0:T(8,128)S(1)} %convolution_select_fusion.12) | copy-start | bytes 3145732
  88.7 17.2 %collective-permute-start.2 = (f32[512,512]{1,0:T(8,128)S(1)}, f32[512,512]{1,0:T(8,128)S(1)}, u32[]{:S(2)}, u32[]{:S(2)}) collective-permute-start(f32[512,512]{1,0:T(8,128)S(1)} %convolution_select_fusion.12), channel_id=1, source_target_pairs={{0,4},{1,5},{2,6},{3,7},{4,8},{5,9},{6,10},{7,11},{8,12},{9,13},{1... | collective-permute-start | bytes 3145736 | tf_op jit(solution)/shard_map/ppermute | solution.py:35
  102.2 27.7 %collective-permute-start.18 = (f32[512,512]{1,0:T(8,128)S(1)}, f32[512,512]{1,0:T(8,128)}, u32[]{:S(2)}, u32[]{:S(2)}) collective-permute-start(f32[512,512]{1,0:T(8,128)S(1)} %fusion), channel_id=1, source_target_pairs={{1,0},{2,1},{3,2},{4,3},{5,4},{6,5},{7,6},{8,7},{9,8},{10,9},{11,1... | collective-permute-start | bytes 3145736 | tf_op jit(solution)/shard_map/ppermute | solution.py:35
  108.8 29.9 %collective-permute-start.3 = (f32[512,512]{1,0:T(8,128)}, f32[512,512]{1,0:T(8,128)}, u32[]{:S(2)}, u32[]{:S(2)}) collective-permute-start(f32[512,512]{1,0:T(8,128)} %convolution_select_fusion.11), channel_id=1, source_target_pairs={{0,8},{1,9},{2,10},{3,11},{4,12},{5,13},{6,14},{7,15},{8,16},{9,17... | collective-permute-start | bytes 3145736 | tf_op jit(solution)/shard_map/ppermute | solution.py:35
  133.0 28.6 %copy-start.1 = (f32[512,512]{1,0:T(8,128)}, f32[512,512]{1,0:T(8,128)S(1)}, u32[]{:S(2)}) copy-start(f32[512,512]{1,0:T(8,128)S(1)} %convolution_select_fusion.6) | copy-start | bytes 3145732
  133.0 28.6 %collective-permute-start.20 = (f32[512,512]{1,0:T(8,128)S(1)}, f32[512,512]{1,0:T(8,128)S(1)}, u32[]{:S(2)}, u32[]{:S(2)}) collective-permute-start(f32[512,512]{1,0:T(8,128)S(1)} %convolution_select_fusion.6), channel_id=1, source_target_pairs={{2,0},{3,1},{4,2},{5,3},{6,4},{7,5},{8,6},{9,7},{10,8},{11,9},{12,... | collective-permute-start | bytes 3145736 | tf_op jit(solution)/shard_map/ppermute | solution.py:35
  142.4 54.6 %copy-start.6 = (f32[512,512]{1,0:T(8,128)}, f32[512,512]{1,0:T(8,128)S(1)}, u32[]{:S(2)}) copy-start(f32[512,512]{1,0:T(8,128)S(1)} %convolution_select_fusion.10) | copy-start | bytes 3145732
  142.4 54.6 %collective-permute-start.4 = (f32[512,512]{1,0:T(8,128)S(1)}, f32[512,512]{1,0:T(8,128)S(1)}, u32[]{:S(2)}, u32[]{:S(2)}) collective-permute-start(f32[512,512]{1,0:T(8,128)S(1)} %convolution_select_fusion.10), channel_id=1, source_target_pairs={{0,16},{1,17},{2,18},{3,19},{4,20},{5,21},{6,22},{7,23},{8,24},{9,... | collective-permute-start | bytes 3145736 | tf_op jit(solution)/shard_map/ppermute | solution.py:35
  150.8 43.2 %copy-start.12 = (f32[512,512]{1,0:T(8,128)S(1)}, f32[512,512]{1,0:T(8,128)}, u32[]{:S(2)}) copy-start(f32[512,512]{1,0:T(8,128)} %copy-done.11) | copy-start | bytes 3145732
  150.8 43.2 %collective-permute-start.7 = (f32[4,512]{1,0:T(4,128)S(1)}, f32[4,512]{1,0:T(4,128)S(1)}, u32[]{:S(2)}, u32[]{:S(2)}) collective-permute-start(f32[4,512]{1,0:T(4,128)S(1)} %fusion.43), channel_id=1, source_target_pairs={{0,1},{1,2},{2,3},{3,4},{4,5},{5,6},{6,7},{7,8},{8,9},{9,10},{10,1... | collective-permute-start | bytes 24584 | tf_op jit(solution)/shard_map/ppermute | solution.py:35
  164.5 70.4 %collective-permute-start.22 = (f32[512,512]{1,0:T(8,128)}, f32[512,512]{1,0:T(8,128)}, u32[]{:S(2)}, u32[]{:S(2)}) collective-permute-start(f32[512,512]{1,0:T(8,128)} %convolution_select_fusion.5), channel_id=1, source_target_pairs={{4,0},{5,1},{6,2},{7,3},{8,4},{9,5},{10,6},{11,7},{12,8},{13,9},{1... | collective-permute-start | bytes 3145736 | tf_op jit(solution)/shard_map/ppermute | solution.py:35
  195.0 8.8 %copy-start.4 = (f32[512,512]{1,0:T(8,128)S(1)}, f32[512,512]{1,0:T(8,128)}, u32[]{:S(2)}) copy-start(f32[512,512]{1,0:T(8,128)} %copy-done.3) | copy-start | bytes 3145732
  195.0 8.8 %collective-permute-start.8 = (f32[4,512]{1,0:T(4,128)S(1)}, f32[4,512]{1,0:T(4,128)S(1)}, u32[]{:S(2)}, u32[]{:S(2)}) collective-permute-start(f32[4,512]{1,0:T(4,128)S(1)} %fusion.42), channel_id=1, source_target_pairs={{0,2},{1,3},{2,4},{3,5},{4,6},{5,7},{6,8},{7,9},{8,10},{9,11},{10,... | collective-permute-start | bytes 24584 | tf_op jit(solution)/shard_map/ppermute | solution.py:35
  200.0 68.0 %collective-permute-start.5 = (f32[512,512]{1,0:T(8,128)}, f32[512,512]{1,0:T(8,128)}, u32[]{:S(2)}, u32[]{:S(2)}) collective-permute-start(f32[512,512]{1,0:T(8,128)} %convolution_select_fusion.9), channel_id=1, source_target_pairs={{0,32},{1,33},{2,34},{3,35},{4,36},{5,37},{6,38},{7,39},{8,40},{9,... | collective-permute-start | bytes 3145736 | tf_op jit(solution)/shard_map/ppermute | solution.py:35
  204.7 5.8 %collective-permute-start.9 = (f32[4,512]{1,0:T(4,128)S(1)}, f32[4,512]{1,0:T(4,128)S(1)}, u32[]{:S(2)}, u32[]{:S(2)}) collective-permute-start(f32[4,512]{1,0:T(4,128)S(1)} %fusion.41), channel_id=1, source_target_pairs={{0,4},{1,5},{2,6},{3,7},{4,8},{5,9},{6,10},{7,11},{8,12},{9,13},{1... | collective-permute-start | bytes 24584 | tf_op jit(solution)/shard_map/ppermute | solution.py:35
  212.7 50.2 %collective-permute-start.10 = (f32[4,512]{1,0:T(4,128)S(1)}, f32[4,512]{1,0:T(4,128)S(1)}, u32[]{:S(2)}, u32[]{:S(2)}) collective-permute-start(f32[4,512]{1,0:T(4,128)S(1)} %fusion.40), channel_id=1, source_target_pairs={{0,8},{1,9},{2,10},{3,11},{4,12},{5,13},{6,14},{7,15},{8,16},{9,17... | collective-permute-start | bytes 24584 | tf_op jit(solution)/shard_map/ppermute | solution.py:35
  239.5 52.3 %collective-permute-start.24 = (f32[512,512]{1,0:T(8,128)}, f32[512,512]{1,0:T(8,128)}, u32[]{:S(2)}, u32[]{:S(2)}) collective-permute-start(f32[512,512]{1,0:T(8,128)} %convolution_select_fusion.4), channel_id=1, source_target_pairs={{8,0},{9,1},{10,2},{11,3},{12,4},{13,5},{14,6},{15,7},{16,8},{17,9... | collective-permute-start | bytes 3145736 | tf_op jit(solution)/shard_map/ppermute | solution.py:35
  265.1 11.1 %copy-start.7 = (f32[512,512]{1,0:T(8,128)S(1)}, f32[512,512]{1,0:T(8,128)}, u32[]{:S(2)}) copy-start(f32[512,512]{1,0:T(8,128)} %copy-done.6) | copy-start | bytes 3145732
  265.1 11.1 %collective-permute-start.11 = (f32[4,512]{1,0:T(4,128)S(1)}, f32[4,512]{1,0:T(4,128)S(1)}, u32[]{:S(2)}, u32[]{:S(2)}) collective-permute-start(f32[4,512]{1,0:T(4,128)S(1)} %fusion.39), channel_id=1, source_target_pairs={{0,16},{1,17},{2,18},{3,19},{4,20},{5,21},{6,22},{7,23},{8,24},{9,... | collective-permute-start | bytes 24584 | tf_op jit(solution)/shard_map/ppermute | solution.py:35
  272.8 29.7 %collective-permute-start.6 = (f32[512,512]{1,0:T(8,128)}, f32[512,512]{1,0:T(8,128)}, u32[]{:S(2)}, u32[]{:S(2)}) collective-permute-start(f32[512,512]{1,0:T(8,128)} %convolution_select_fusion.8), channel_id=1, source_target_pairs={{0,64},{1,65},{2,66},{3,67},{4,68},{5,69},{6,70},{7,71},{8,72},{9,... | collective-permute-start | bytes 3145736 | tf_op jit(solution)/shard_map/ppermute | solution.py:35
  277.2 10.5 %collective-permute-start.12 = (f32[4,512]{1,0:T(4,128)S(1)}, f32[4,512]{1,0:T(4,128)S(1)}, u32[]{:S(2)}, u32[]{:S(2)}) collective-permute-start(f32[4,512]{1,0:T(4,128)S(1)} %fusion.38), channel_id=1, source_target_pairs={{0,32},{1,33},{2,34},{3,35},{4,36},{5,37},{6,38},{7,39},{8,40},{9,... | collective-permute-start | bytes 24584 | tf_op jit(solution)/shard_map/ppermute | solution.py:35
  289.8 10.5 %collective-permute-start.13 = (f32[4,512]{1,0:T(4,128)S(1)}, f32[4,512]{1,0:T(4,128)S(1)}, u32[]{:S(2)}, u32[]{:S(2)}) collective-permute-start(f32[4,512]{1,0:T(4,128)S(1)} %fusion.37), channel_id=1, source_target_pairs={{0,64},{1,65},{2,66},{3,67},{4,68},{5,69},{6,70},{7,71},{8,72},{9,... | collective-permute-start | bytes 24584 | tf_op jit(solution)/shard_map/ppermute | solution.py:35
  296.5 49.3 %collective-permute-start.26 = (f32[512,512]{1,0:T(8,128)}, f32[512,512]{1,0:T(8,128)}, u32[]{:S(2)}, u32[]{:S(2)}) collective-permute-start(f32[512,512]{1,0:T(8,128)} %convolution_select_fusion.3), channel_id=1, source_target_pairs={{16,0},{17,1},{18,2},{19,3},{20,4},{21,5},{22,6},{23,7},{24,8},{25... | collective-permute-start | bytes 3145736 | tf_op jit(solution)/shard_map/ppermute | solution.py:35
  302.5 4.8 copy-start.13
  306.3 1.0 copy-start.10
  308.3 4.5 collective-permute-start.14
  315.0 87.7 %collective-permute-start.15 = (f32[4,512]{1,0:T(4,128)S(1)}, f32[4,512]{1,0:T(4,128)S(1)}, u32[]{:S(2)}, u32[]{:S(2)}) collective-permute-start(f32[4,512]{1,0:T(4,128)S(1)} %fusion.35), channel_id=1, source_target_pairs={{0,1},{1,2},{2,3},{3,4},{4,5},{5,6},{6,7},{7,8},{8,9},{9,10},{10,1... | collective-permute-start | bytes 24584 | tf_op jit(solution)/shard_map/ppermute | solution.py:35
  350.5 79.3 %collective-permute-start.28 = (f32[512,512]{1,0:T(8,128)}, f32[512,512]{1,0:T(8,128)}, u32[]{:S(2)}, u32[]{:S(2)}) collective-permute-start(f32[512,512]{1,0:T(8,128)} %convolution_select_fusion.2), channel_id=1, source_target_pairs={{32,0},{33,1},{34,2},{35,3},{36,4},{37,5},{38,6},{39,7},{40,8},{41... | collective-permute-start | bytes 3145736 | tf_op jit(solution)/shard_map/ppermute | solution.py:35
  412.0 14.9 %copy-start.2 = (f32[512,512]{1,0:T(8,128)S(1)}, f32[512,512]{1,0:T(8,128)}, u32[]{:S(2)}) copy-start(f32[512,512]{1,0:T(8,128)} %copy-done.1) | copy-start | bytes 3145732
  413.4 5.5 %collective-permute-start.16 = (f32[4,512]{1,0:T(4,128)S(1)}, f32[4,512]{1,0:T(4,128)S(1)}, u32[]{:S(2)}, u32[]{:S(2)}) collective-permute-start(f32[4,512]{1,0:T(4,128)S(1)} %fusion.23), channel_id=1, source_target_pairs={{1,0},{2,1},{3,2},{4,3},{5,4},{6,5},{7,6},{8,7},{9,8},{10,9},{11,1... | collective-permute-start | bytes 24584 | tf_op jit(solution)/shard_map/ppermute | solution.py:35
  419.9 7.1 %collective-permute-start.17 = (f32[4,512]{1,0:T(4,128)S(1)}, f32[4,512]{1,0:T(4,128)S(1)}, u32[]{:S(2)}, u32[]{:S(2)}) collective-permute-start(f32[4,512]{1,0:T(4,128)S(1)} %fusion.21), channel_id=1, source_target_pairs={{2,0},{3,1},{4,2},{5,3},{6,4},{7,5},{8,6},{9,7},{10,8},{11,9},{12,... | collective-permute-start | bytes 24584 | tf_op jit(solution)/shard_map/ppermute | solution.py:35
  427.9 7.9 %collective-permute-start.19 = (f32[4,512]{1,0:T(4,128)S(1)}, f32[4,512]{1,0:T(4,128)S(1)}, u32[]{:S(2)}, u32[]{:S(2)}) collective-permute-start(f32[4,512]{1,0:T(4,128)S(1)} %fusion.20), channel_id=1, source_target_pairs={{4,0},{5,1},{6,2},{7,3},{8,4},{9,5},{10,6},{11,7},{12,8},{13,9},{1... | collective-permute-start | bytes 24584 | tf_op jit(solution)/shard_map/ppermute | solution.py:35
  433.6 41.4 %collective-permute-start.30 = (f32[512,512]{1,0:T(8,128)S(1)}, f32[512,512]{1,0:T(8,128)S(1)}, u32[]{:S(2)}, u32[]{:S(2)}) collective-permute-start(f32[512,512]{1,0:T(8,128)S(1)} %convolution_select_fusion.1), channel_id=1, source_target_pairs={{64,0},{65,1},{66,2},{67,3},{68,4},{69,5},{70,6},{71,7},{72,8},{73... | collective-permute-start | bytes 3145736 | tf_op jit(solution)/shard_map/ppermute | solution.py:35
  438.0 5.5 %collective-permute-start.21 = (f32[4,512]{1,0:T(4,128)S(1)}, f32[4,512]{1,0:T(4,128)S(1)}, u32[]{:S(2)}, u32[]{:S(2)}) collective-permute-start(f32[4,512]{1,0:T(4,128)S(1)} %fusion.19), channel_id=1, source_target_pairs={{8,0},{9,1},{10,2},{11,3},{12,4},{13,5},{14,6},{15,7},{16,8},{17,9... | collective-permute-start | bytes 24584 | tf_op jit(solution)/shard_map/ppermute | solution.py:35
  445.7 7.7 %collective-permute-start.23 = (f32[4,512]{1,0:T(4,128)S(1)}, f32[4,512]{1,0:T(4,128)S(1)}, u32[]{:S(2)}, u32[]{:S(2)}) collective-permute-start(f32[4,512]{1,0:T(4,128)S(1)} %fusion.18), channel_id=1, source_target_pairs={{16,0},{17,1},{18,2},{19,3},{20,4},{21,5},{22,6},{23,7},{24,8},{25... | collective-permute-start | bytes 24584 | tf_op jit(solution)/shard_map/ppermute | solution.py:35
  455.6 9.5 %collective-permute-start.25 = (f32[4,512]{1,0:T(4,128)S(1)}, f32[4,512]{1,0:T(4,128)S(1)}, u32[]{:S(2)}, u32[]{:S(2)}) collective-permute-start(f32[4,512]{1,0:T(4,128)S(1)} %fusion.17), channel_id=1, source_target_pairs={{32,0},{33,1},{34,2},{35,3},{36,4},{37,5},{38,6},{39,7},{40,8},{41... | collective-permute-start | bytes 24584 | tf_op jit(solution)/shard_map/ppermute | solution.py:35
  467.2 5.5 %collective-permute-start.27 = (f32[4,512]{1,0:T(4,128)S(1)}, f32[4,512]{1,0:T(4,128)S(1)}, u32[]{:S(2)}, u32[]{:S(2)}) collective-permute-start(f32[4,512]{1,0:T(4,128)S(1)} %fusion.16), channel_id=1, source_target_pairs={{64,0},{65,1},{66,2},{67,3},{68,4},{69,5},{70,6},{71,7},{72,8},{73... | collective-permute-start | bytes 24584 | tf_op jit(solution)/shard_map/ppermute | solution.py:35
  473.7 7.1 %collective-permute-start.29 = (f32[4,512]{1,0:T(4,128)S(1)}, f32[4,512]{1,0:T(4,128)S(1)}, u32[]{:S(2)}, u32[]{:S(2)}) collective-permute-start(f32[4,512]{1,0:T(4,128)S(1)} %fusion.15), channel_id=1, source_target_pairs={{128,0},{129,1},{130,2},{131,3},{132,4},{133,5},{134,6},{135,7},{1... | collective-permute-start | bytes 24584 | tf_op jit(solution)/shard_map/ppermute | solution.py:35
  481.7 5.5 %collective-permute-start.31 = (f32[4,512]{1,0:T(4,128)S(1)}, f32[4,512]{1,0:T(4,128)S(1)}, u32[]{:S(2)}, u32[]{:S(2)}) collective-permute-start(f32[4,512]{1,0:T(4,128)S(1)} %fusion.14), channel_id=1, source_target_pairs={{1,0},{2,1},{3,2},{4,3},{5,4},{6,5},{7,6},{8,7},{9,8},{10,9},{11,1... | collective-permute-start | bytes 24584 | tf_op jit(solution)/shard_map/ppermute | solution.py:35
